TPU v7x, 512 devices: a whole 4x4x16 slice. The times are simulated.
512 devices in a mesh: dp: 32 (over x, y, core), expert: 16 (over z).
Axes of the slice: x: 4, y: 4, z: 16, core: 2. Of those that a mesh axis runs over, the one named last changes fastest.
Arguments:
- tokens: bfloat16 [4096, 2048], P('dp', 'expert'), may hold values from -6 to 6
- route_weight: bfloat16 [4096, 8], P('dp'), may hold values from 0.049804688 to 0.44921875
- expert_ids: int32 [4096, 8], P('dp'), may hold values from 0 to 127, all different within a row; in each aligned block of 128 rows (0 to 127, 128 to 255, ...) at most 16 rows name the same one
- gate_weight: bfloat16 [16, 6144, 2048], P('expert', 'dp'), may hold values from -0.125 to 0.125
- up_weight: bfloat16 [16, 6144, 2048], P('expert', 'dp'), may hold values from -0.125 to 0.125
- down_weight: bfloat16 [16, 6144, 2048], P('expert', 'dp'), may hold values from -0.21875 to 0.21875
- grad_output: bfloat16 [4096, 2048], P('dp', 'expert'), may hold values from -1.75 to 1.75
Outputs:
- mixed: bfloat16 [4096, 2048], P('dp', 'expert')
- grad_tokens: bfloat16 [4096, 2048], P('dp', 'expert')
- grad_route: float32 [4096, 8], P(('dp', 'expert'))
- grad_gate: bfloat16 [16, 6144, 2048], P('expert', 'dp')
- grad_up: bfloat16 [16, 6144, 2048], P('expert', 'dp')
- grad_down: bfloat16 [16, 6144, 2048], P('expert', 'dp')
Inputs may be any that keep to these rules, and one draw needn't show every extreme that they name: `expert_ids`: each token names 8 different experts; among the 128 tokens of one device's aligned block no expert is named more than 16 times, a bound that some block reaches.
All inputs are finite; a program needn't handle non-finite values.
Results may differ from a plain program's by a relative error of at most 0.015.
Values may be sent and summed in bfloat16 or wider, within the bound.
No kernel may reach another device: no remote copies, remote signals or barrier semaphores. Data moves between devices by JAX's collectives and lax.ppermute only.
A program may use at most 64 MiB of HBM per device.

v0:
```python
import jax
import jax.numpy as jnp
from jax import lax
from jax.sharding import PartitionSpec as P

PIECES = 4


def contract_last(left_side, right_side):
    return lax.dot_general(
        left_side, right_side, (((1,), (1,)), ((), ())), preferred_element_type=jnp.float32
    )


def contract_first(left_side, right_side):
    return lax.dot_general(
        left_side, right_side, (((0,), (0,)), ((), ())), preferred_element_type=jnp.float32
    )


def silu_parts(gate_act):
    sigmoid_val = jax.nn.sigmoid(gate_act)
    return (gate_act * sigmoid_val, sigmoid_val * (1.0 + gate_act * (1.0 - sigmoid_val)))


def expert_forward(slot_rows, slot_scale, gate_piece, up_piece, down_piece):
    gate_act = contract_last(slot_rows, gate_piece)
    up_act = contract_last(slot_rows, up_piece)
    active, silu_slope = silu_parts(gate_act)
    hidden = (active * up_act).astype(jnp.bfloat16)
    partial_out = jnp.dot(hidden, down_piece, preferred_element_type=jnp.float32)
    scaled = (slot_scale.astype(jnp.float32)[:, None] * partial_out).astype(jnp.bfloat16)
    return (scaled, gate_act, up_act, hidden)


def on_device(tokens, route_weight, expert_ids, gate_weight, up_weight, down_weight, grad_output):
    groups = lax.axis_size("expert")
    group_index = lax.axis_index("expert")
    data_size = lax.axis_size("dp")
    exp_local = data_size // PIECES
    tok_local, topk_count = expert_ids.shape
    capacity = min(tok_local, 2 * tok_local * topk_count // (exp_local * groups))
    full_tokens, full_grad = (
        lax.all_gather(tokens, "expert", axis=1, tiled=True),
        lax.all_gather(grad_output, "expert", axis=1, tiled=True),
    )
    feature_width = full_tokens.shape[1]
    gate_piece = gate_weight[0]
    up_piece = up_weight[0]
    down_piece = down_weight[0]
    flat_ids = expert_ids.reshape(-1)
    row_count = flat_ids.shape[0]
    owned_rows = flat_ids // exp_local == group_index
    local_ids = flat_ids % exp_local
    chosen = (
        (local_ids[:, None] == jnp.arange(exp_local, dtype=jnp.int32)[None, :])
        & owned_rows[:, None]
    ).astype(jnp.int32)
    slot_ranks = jnp.sum(chosen * (jnp.cumsum(chosen, axis=0) - 1), axis=1)
    slot_count = exp_local * capacity
    slot_pos = jnp.where(owned_rows, local_ids * capacity + slot_ranks, slot_count)
    row_index = jnp.arange(row_count, dtype=jnp.int32)
    row_of = jnp.zeros((slot_count,), jnp.int32).at[slot_pos].set(row_index, mode="drop")
    slot_live = (
        jnp.zeros((slot_count,), jnp.int32).at[slot_pos].set(jnp.ones_like(row_index), mode="drop")
    )
    token_of = row_of // topk_count
    keep_mask = slot_live.astype(tokens.dtype)[:, None]
    slot_weight = route_weight.reshape(-1)[row_of] * slot_live.astype(route_weight.dtype)

    def spread(values):
        trailing = values.shape[1:]
        grouped = values.reshape((exp_local, 1, capacity) + trailing)
        return jnp.broadcast_to(grouped, (exp_local, PIECES, capacity) + trailing).reshape(
            (data_size, capacity) + trailing
        )

    send_rows = spread(full_tokens[token_of] * keep_mask)
    send_weight = spread(slot_weight)
    send_grads = spread(full_grad[token_of] * keep_mask)
    recv_grads = None
    recv_scale = None
    recv_rows, recv_weight = (
        lax.all_to_all(send_rows, "dp", split_axis=0, concat_axis=0, tiled=True),
        lax.all_to_all(send_weight, "dp", split_axis=0, concat_axis=0, tiled=True),
    )
    scaled, gate_act, up_act, hidden = expert_forward(
        recv_rows.reshape(-1, feature_width),
        recv_weight.reshape(-1),
        gate_piece,
        up_piece,
        down_piece,
    )
    returned = lax.all_to_all(
        scaled.reshape(data_size, capacity, feature_width),
        "dp",
        split_axis=0,
        concat_axis=0,
        tiled=True,
    )
    slot_rows = recv_rows.reshape(-1, feature_width)
    wide_token = spread(token_of).reshape(-1)
    wide_live = spread(slot_live).reshape(-1)
    wide_row = spread(row_of).reshape(-1)
    token_place = (
        (wide_token[None, :] == jnp.arange(tok_local, dtype=jnp.int32)[:, None])
        & (wide_live[None, :] > 0)
    ).astype(jnp.bfloat16)
    mixed_sum = jnp.dot(
        token_place, returned.reshape(-1, feature_width), preferred_element_type=jnp.float32
    )
    recv_grads, recv_scale = (
        lax.all_to_all(send_grads, "dp", split_axis=0, concat_axis=0, tiled=True),
        lax.all_to_all(send_weight, "dp", split_axis=0, concat_axis=0, tiled=True),
    )
    active, silu_slope = silu_parts(gate_act)
    slot_grads = recv_grads.reshape(-1, feature_width)
    weight_wide = recv_scale.reshape(-1).astype(jnp.float32)[:, None]
    into_hidden = contract_last(slot_grads, down_piece)
    route_terms = jnp.sum(into_hidden * hidden.astype(jnp.float32), axis=1).astype(jnp.bfloat16)
    hidden_grad = weight_wide * into_hidden
    gate_grad = (hidden_grad * up_act * silu_slope).astype(jnp.bfloat16)
    up_grad = (hidden_grad * active).astype(jnp.bfloat16)
    row_grad = (
        jnp.dot(gate_grad, gate_piece, preferred_element_type=jnp.float32)
        + jnp.dot(up_grad, up_piece, preferred_element_type=jnp.float32)
    ).astype(jnp.bfloat16)
    scaled_grad = (weight_wide * slot_grads.astype(jnp.float32)).astype(jnp.bfloat16)
    grad_gate = contract_first(gate_grad, slot_rows).astype(jnp.bfloat16)[None]
    grad_up = contract_first(up_grad, slot_rows).astype(jnp.bfloat16)[None]
    grad_down = contract_first(hidden, scaled_grad).astype(jnp.bfloat16)[None]
    back_rows, back_terms = (
        lax.all_to_all(
            row_grad.reshape(data_size, capacity, feature_width),
            "dp",
            split_axis=0,
            concat_axis=0,
            tiled=True,
        ),
        lax.all_to_all(
            route_terms.reshape(data_size, capacity), "dp", split_axis=0, concat_axis=0, tiled=True
        ),
    )
    token_sum = jnp.dot(
        token_place, back_rows.reshape(-1, feature_width), preferred_element_type=jnp.float32
    )
    row_place = (
        (wide_row[None, :] == jnp.arange(row_count, dtype=jnp.int32)[:, None])
        & (wide_live[None, :] > 0)
    ).astype(jnp.bfloat16)
    route_sum = jnp.dot(
        row_place, back_terms.reshape(-1), preferred_element_type=jnp.float32
    ).reshape(tok_local, topk_count)
    mixed_part, token_part, route_part = (
        lax.psum_scatter(mixed_sum, "expert", scatter_dimension=1, tiled=True),
        lax.psum_scatter(token_sum, "expert", scatter_dimension=1, tiled=True),
        lax.psum_scatter(route_sum, "expert", scatter_dimension=0, tiled=True),
    )
    return (
        mixed_part.astype(jnp.bfloat16),
        token_part.astype(jnp.bfloat16),
        route_part,
        grad_gate,
        grad_up,
        grad_down,
    )


def solution(mesh):
    return jax.shard_map(
        on_device,
        mesh=mesh,
        in_specs=(
            P("dp", "expert"),
            P("dp", None),
            P("dp", None),
            P("expert", "dp", None),
            P("expert", "dp", None),
            P("expert", "dp", None),
            P("dp", "expert"),
        ),
        out_specs=(
            P("dp", "expert"),
            P("dp", "expert"),
            P(("dp", "expert"), None),
            P("expert", "dp", None),
            P("expert", "dp", None),
            P("expert", "dp", None),
        ),
        check_vma=False,
    )
```

profile of v0, /device:TPU:2, one launch (start us, length us, event | category | flops | bytes accessed | tf_op | source)
XLA Modules:
  0.0 366.5 jit_solution(7416273939957925832)
XLA Ops:
  9.3 2.3 reduce-window.6
  12.2 4.3 %scatter_custom_fusion.1 = s32[128]{0:T(128)S(1)} fusion(s32[1024]{0:T(1024)S(1)} %bitcast.84, s32[1024]{0:T(1024)S(1)} %ne.90, s32[]{:T(128)} %constant.53.clone.1), kind=kCustom, calls=%fused_computation.95 | custom fusion | bytes 516 | tf_op jit(solution)/shard_map/scatter | solution.py:65
  16.5 4.3 %scatter_custom_fusion = s32[128]{0:T(128)S(1)} fusion(s32[1024]{0:T(1024)S(1)} %bitcast.85, s32[1024]{0:T(1024)S(1)} %iota.26, s32[]{:T(128)} %constant.53.clone.1), kind=kCustom, calls=%fused_computation.97 | custom fusion | bytes 516 | tf_op jit(solution)/shard_map/scatter | solution.py:63
  22.9 9.4 %all-to-all-start = ((bf16[32,1,16]{2,1,0:T(2,128)(2,1)}), bf16[32,1,16]{2,1,0:T(2,128)(2,1)S(1)}, u32[]{:S(2)}, u32[]{:S(2)}) async-start(bf16[32,1,16]{2,1,0:T(2,128)(2,1)} %copy.26), calls=%async_computation | async-start | bytes 32768 | tf_op jit(solution)/shard_map/all_to_all | solution.py:85
  32.4 37.0 %all_gather.6 = bf16[128,2048]{1,0:T(8,128)(2,1)S(1)} all-gather(bf16[128,128]{1,0:T(8,128)(2,1)} %param.7), channel_id=1, replica_groups=mesh['dp'=32,'expert'=16] {'expert'}, dimensions={1}, use_global_device_ids=true | all-gather | bytes 557056 | tf_op jit(solution)/shard_map/all_gather | solution.py:44
  69.4 29.3 %all_gather.7 = bf16[128,2048]{1,0:T(8,128)(2,1)S(1)} all-gather(bf16[128,128]{1,0:T(8,128)(2,1)} %param.13), channel_id=1, replica_groups=mesh['dp'=32,'expert'=16] {'expert'}, dimensions={1}, use_global_device_ids=true | all-gather | bytes 557056 | tf_op jit(solution)/shard_map/all_gather | solution.py:45
  101.0 32.6 %all_to_all.36 = bf16[32,16,2048]{2,1,0:T(8,128)(2,1)S(1)} all-to-all(bf16[32,16,2048]{2,1,0:T(8,128)(2,1)S(1)} %bitcast.76), channel_id=1, replica_groups=mesh['dp'=32,'expert'=16] {'dp'}, dimensions={0} | all-to-all | bytes 4194304 | tf_op jit(solution)/shard_map/all_to_all | solution.py:84
  135.2 7.0 %all-to-all-start.3 = ((bf16[32,16,2048]{2,1,0:T(8,128)(2,1)}), bf16[32,16,2048]{2,1,0:T(8,128)(2,1)}, u32[]{:S(2)}, u32[]{:S(2)}) async-start(bf16[32,16,2048]{2,1,0:T(8,128)(2,1)} %bitcast.75), calls=%async_computation.4 | async-start | bytes 4194304 | tf_op jit(solution)/shard_map/all_to_all | solution.py:113
  142.3 2.8 fusion.12
  146.7 21.4 %all-to-all-done.3 = bf16[32,16,2048]{2,1,0:T(8,128)(2,1)} async-done(((bf16[32,16,2048]{2,1,0:T(8,128)(2,1)}), bf16[32,16,2048]{2,1,0:T(8,128)(2,1)}, u32[]{:S(2)}, u32[]{:S(2)}) %all-to-all-start.3) | async-done | bytes 2097184 | tf_op jit(solution)/shard_map/all_to_all | solution.py:113
  168.1 2.7 multiply_reduce_fusion
  171.5 2.0 multiply_convert_fusion.1
  173.6 7.7 %all-to-all-start.2 = ((bf16[32,16,2048]{2,1,0:T(8,128)(2,1)}), bf16[32,16,2048]{2,1,0:T(8,128)(2,1)}, u32[]{:S(2)}, u32[]{:S(2)}) async-start(bf16[32,16,2048]{2,1,0:T(8,128)(2,1)} %bitcast.79), calls=%async_computation.2 | async-start | bytes 4194304 | tf_op jit(solution)/shard_map/all_to_all | solution.py:94
  183.6 2.1 add_convert_fusion
  185.7 21.5 %all-to-all-done.2 = bf16[32,16,2048]{2,1,0:T(8,128)(2,1)} async-done(((bf16[32,16,2048]{2,1,0:T(8,128)(2,1)}), bf16[32,16,2048]{2,1,0:T(8,128)(2,1)}, u32[]{:S(2)}, u32[]{:S(2)}) %all-to-all-start.2) | async-done | bytes 2097184 | tf_op jit(solution)/shard_map/all_to_all | solution.py:94
  207.2 7.7 %all-to-all-start.4 = ((bf16[32,16,2048]{2,1,0:T(8,128)(2,1)}), bf16[32,16,2048]{2,1,0:T(8,128)(2,1)}, u32[]{:S(2)}, u32[]{:S(2)}) async-start(bf16[32,16,2048]{2,1,0:T(8,128)(2,1)} %bitcast.74), calls=%async_computation.5 | async-start | bytes 4194304 | tf_op jit(solution)/shard_map/all_to_all | solution.py:133
  215.0 3.1 fusion.22
  218.3 22.6 %all-to-all-done.4 = bf16[32,16,2048]{2,1,0:T(8,128)(2,1)} async-done(((bf16[32,16,2048]{2,1,0:T(8,128)(2,1)}), bf16[32,16,2048]{2,1,0:T(8,128)(2,1)}, u32[]{:S(2)}, u32[]{:S(2)}) %all-to-all-start.4) | async-done | bytes 2097184 | tf_op jit(solution)/shard_map/all_to_all | solution.py:133
  240.9 3.0 fusion.20
  246.8 6.8 %all-to-all-start.5 = ((bf16[32,1,16]{2,1,0:T(2,128)(2,1)}), bf16[32,1,16]{2,1,0:T(2,128)(2,1)S(1)}, u32[]{:S(2)}, u32[]{:S(2)}) async-start(bf16[32,1,16]{2,1,0:T(2,128)(2,1)} %convert_element_type.95), calls=%async_computation.7 | async-start | bytes 32768 | tf_op jit(solution)/shard_map/all_to_all | solution.py:140
  255.1 3.2 fusion.2
  259.9 2.5 fusion.4
  262.4 54.3 %all-reduce = f32[128,8]{1,0:T(8,128)S(1)} all-reduce(f32[128,8]{1,0:T(8,128)S(1)} %bitcast.80), channel_id=4, replica_groups=mesh['dp'=32,'expert'=16] {'expert'}, use_global_device_ids=true, to_apply=%region_8.9.clone | all-reduce | flops 1024 | bytes 8192
  318.7 39.4 %reduce-scatter.5.cloned.1.call-done = f32[128,128]{1,0:T(8,128)} async-done(((f32[128,2048]{1,0:T(8,128)}), f32[128,128]{1,0:T(8,128)}) %reduce-scatter.5.cloned.1.call-update) | async-done | bytes 65552 | tf_op jit(solution)/shard_map/reduce_scatter | solution.py:156
  (74 shorter events, 22.5 us)
Async XLA Ops:
  7.2 161.0 %copy-start = (bf16[1,192,2048]{2,1,0:T(8,128)(2,1)S(1)}, bf16[1,192,2048]{2,1,0:T(8,128)(2,1)}, u32[]{:S(2)}) copy-start(bf16[1,192,2048]{2,1,0:T(8,128)(2,1)} %param.12) | copy-start | bytes 2359300
  22.9 77.9 %all-to-all-start = ((bf16[32,1,16]{2,1,0:T(2,128)(2,1)}), bf16[32,1,16]{2,1,0:T(2,128)(2,1)S(1)}, u32[]{:S(2)}, u32[]{:S(2)}) async-start(bf16[32,1,16]{2,1,0:T(2,128)(2,1)} %copy.26), calls=%async_computation | async-start | bytes 32768 | tf_op jit(solution)/shard_map/all_to_all | solution.py:85
  135.2 33.0 %all-to-all-start.3 = ((bf16[32,16,2048]{2,1,0:T(8,128)(2,1)}), bf16[32,16,2048]{2,1,0:T(8,128)(2,1)}, u32[]{:S(2)}, u32[]{:S(2)}) async-start(bf16[32,16,2048]{2,1,0:T(8,128)(2,1)} %bitcast.75), calls=%async_computation.4 | async-start | bytes 4194304 | tf_op jit(solution)/shard_map/all_to_all | solution.py:113
  142.3 2.8 copy-start.1
  170.9 0.7 copy-start.3
  173.6 33.6 %all-to-all-start.2 = ((bf16[32,16,2048]{2,1,0:T(8,128)(2,1)}), bf16[32,16,2048]{2,1,0:T(8,128)(2,1)}, u32[]{:S(2)}, u32[]{:S(2)}) async-start(bf16[32,16,2048]{2,1,0:T(8,128)(2,1)} %bitcast.79), calls=%async_computation.2 | async-start | bytes 4194304 | tf_op jit(solution)/shard_map/all_to_all | solution.py:94
  181.7 2.0 copy-start.2
  207.2 33.6 %all-to-all-start.4 = ((bf16[32,16,2048]{2,1,0:T(8,128)(2,1)}), bf16[32,16,2048]{2,1,0:T(8,128)(2,1)}, u32[]{:S(2)}, u32[]{:S(2)}) async-start(bf16[32,16,2048]{2,1,0:T(8,128)(2,1)} %bitcast.74), calls=%async_computation.5 | async-start | bytes 4194304 | tf_op jit(solution)/shard_map/all_to_all | solution.py:133
  214.9 102.4 %reduce-scatter.3.cloned.1.call-start = ((), (), s32[]{:S(2)}) async-start(), calls=%async_computation.8 | async-start | bytes 1114112 | tf_op jit(solution)/shard_map/reduce_scatter | solution.py:155
  218.1 140.1 %reduce-scatter.5.cloned.1.call-start = ((), (), s32[]{:S(2)}) async-start(), calls=%async_computation.9 | async-start | bytes 1114112 | tf_op jit(solution)/shard_map/reduce_scatter | solution.py:156
  246.8 13.0 %all-to-all-start.5 = ((bf16[32,1,16]{2,1,0:T(2,128)(2,1)}), bf16[32,1,16]{2,1,0:T(2,128)(2,1)S(1)}, u32[]{:S(2)}, u32[]{:S(2)}) async-start(bf16[32,1,16]{2,1,0:T(2,128)(2,1)} %convert_element_type.95), calls=%async_computation.7 | async-start | bytes 32768 | tf_op jit(solution)/shard_map/all_to_all | solution.py:140
  253.6 1.5 copy-start.4
Sparse Core Ops, SparseCore 0:
  218.5 67.8 reduce-scatter.2
  289.3 68.8 reduce-scatter.4
where the time goes:
time: 367 us; the launch traced here: 366 us
  blocking collectives  153 us (42%)
  waiting for transfers between devices  105 us (29%)
  starting transfers between devices  38.9 us (11%)
  matrix products  27.9 us (8%)
  local copies, waits for them, and re-layouts  20.7 us (6%)
  between operations  15 us (4%)
  other arithmetic  5.84 us (2%)
    unnamed x1, blocking collectives  54.3 us
    reduce_scatter x1, waiting for transfers between devices, on_device(): lax.psum_scatter(token_sum, 'expert', scatter_dimension=1, tiled=True)  39.4 us
    all_gather x1, blocking collectives, on_device(): lax.all_gather(tokens, 'expert', axis=1, tiled=True)  37 us
    all_to_all x1, blocking collectives, on_device(): lax.all_to_all(send_rows, 'dp', split_axis=0, concat_axis=0, tiled=True)  32.6 us
    all_gather x1, blocking collectives, on_device(): lax.all_gather(grad_output, 'expert', axis=1, tiled=True)  29.3 us
    all_to_all x1, waiting for transfers between devices, on_device(): lax.all_to_all(row_grad.reshape(data_size, capacity, feature_width), 'dp'...  22.6 us
    all_to_all x1, waiting for transfers between devices, on_device(): lax.all_to_all(scaled.reshape(data_size, capacity, feature_width), 'dp',...  21.5 us
    all_to_all x1, waiting for transfers between devices, on_device(): lax.all_to_all(send_grads, 'dp', split_axis=0, concat_axis=0, tiled=True)  21.4 us
  transfers between devices with their start and end apart: 7, of which 5 were waited for; matrix products, arithmetic and copies ran while one was open for 8% of the time, Pallas kernels for 0%

commit v1 on v0

--- a/solution.py
+++ b/solution.py
@@ -4,6 +4,24 @@
 from jax.sharding import PartitionSpec as P
 
 PIECES = 4
+
+
+def gather_around(value, axis, dim):
+    ways, here, hop = (lax.axis_size(axis), lax.axis_index(axis), value.shape[dim])
+    shape = [n * ways if d == dim else n for d, n in enumerate(value.shape)]
+    full = lax.dynamic_update_slice_in_dim(
+        jnp.zeros(shape, value.dtype), value, here * hop, axis=dim
+    )
+    going_up = going_down = value
+    for far in range(1, ways // 2 + 1):
+        going_up = lax.ppermute(going_up, axis, [(d, (d + 1) % ways) for d in range(ways)])
+        full = lax.dynamic_update_slice_in_dim(full, going_up, (here - far) % ways * hop, axis=dim)
+        if 2 * far < ways:
+            going_down = lax.ppermute(going_down, axis, [(d, (d - 1) % ways) for d in range(ways)])
+            full = lax.dynamic_update_slice_in_dim(
+                full, going_down, (here + far) % ways * hop, axis=dim
+            )
+    return full
 
 
 def contract_last(left_side, right_side):
@@ -42,7 +60,7 @@
     capacity = min(tok_local, 2 * tok_local * topk_count // (exp_local * groups))
     full_tokens, full_grad = (
         lax.all_gather(tokens, "expert", axis=1, tiled=True),
-        lax.all_gather(grad_output, "expert", axis=1, tiled=True),
+        gather_around(grad_output, "expert", 1),
     )
     feature_width = full_tokens.shape[1]
     gate_piece = gate_weight[0]

time: 367 us -> 397 us (1.082)
  starting transfers between devices: 38.9 us -> 91.3 us
  blocking collectives: 153 us -> 118 us
  waiting for transfers between devices: 105 us -> 116 us
    ppermute x0 -> x15, starting transfers between devices: none -> 54.5 us  [the longest x7 36.3 us: gather_around(): lax.ppermute(going_down, axis, [(d, (d - 1) % ways) for d in range(ways)])]
    all_gather x1 -> x0, blocking collectives: 29.3 us -> none  [on_device(): lax.all_gather(grad_output, 'expert', axis=1, tiled=True)]
    ppermute x0 -> x15, waiting for transfers between devices: none -> 10.1 us  [the longest x8 10.1 us: gather_around(): lax.ppermute(going_up, axis, [(d, (d + 1) % ways) for d in range(ways)])]
    all_gather x1, blocking collectives: 37 us -> 32.4 us  [on_device(): lax.all_gather(tokens, 'expert', axis=1, tiled=True)]
  transfers between devices with their start and end apart: 7 -> 22, of which waited for: 5 -> 7; matrix products, arithmetic and copies ran while one was open for 8% -> 12% of each run, Pallas kernels for 0% -> 0%
where the time goes in v1:
time: 397 us; the launch traced here: 396 us
  blocking collectives  118 us (30%)
  waiting for transfers between devices  116 us (29%)
  starting transfers between devices  91.3 us (23%)
  matrix products  27.9 us (7%)
  local copies, waits for them, and re-layouts  20.9 us (5%)
  between operations  15.6 us (4%)
  other arithmetic  5.84 us (1%)
    unnamed x1, blocking collectives  52.7 us
    reduce_scatter x1, waiting for transfers between devices, on_device(): lax.psum_scatter(token_sum, 'expert', scatter_dimension=1, tiled=True)  40.3 us
    ppermute x7, starting transfers between devices, gather_around(): lax.ppermute(going_down, axis, [(d, (d - 1) % ways) for d in range(ways)])  36.3 us
    all_to_all x1, blocking collectives, on_device(): lax.all_to_all(send_rows, 'dp', split_axis=0, concat_axis=0, tiled=True)  32.6 us
    all_gather x1, blocking collectives, on_device(): lax.all_gather(tokens, 'expert', axis=1, tiled=True)  32.4 us
    all_to_all x1, waiting for transfers between devices, on_device(): lax.all_to_all(row_grad.reshape(data_size, capacity, feature_width), 'dp'...  22.8 us
    all_to_all x1, waiting for transfers between devices, on_device(): lax.all_to_all(scaled.reshape(data_size, capacity, feature_width), 'dp',...  21.6 us
    all_to_all x1, waiting for transfers between devices, on_device(): lax.all_to_all(send_grads, 'dp', split_axis=0, concat_axis=0, tiled=True)  21.4 us
  transfers between devices with their start and end apart: 22, of which 7 were waited for; matrix products, arithmetic and copies ran while one was open for 12% of the time, Pallas kernels for 0%

profile of v1, /device:TPU:2, one launch (start us, length us, event | category | flops | bytes accessed | tf_op | source)
XLA Modules:
  0.0 395.6 jit_solution(13964038984249857254)
XLA Ops:
  7.2 11.5 %collective-permute-start.1 = (bf16[128,128]{1,0:T(8,128)(2,1)}, bf16[128,128]{1,0:T(8,128)(2,1)S(1)}, u32[]{:S(2)}, u32[]{:S(2)}) collective-permute-start(bf16[128,128]{1,0:T(8,128)(2,1)} %param.13), channel_id=1, source_target_pairs={{0,15},{1,0},{2,1},{3,2},{4,3},{5,4},{6,5},{7,6},{8,7},{9,8},{10,9... | collective-permute-start | bytes 98312 | tf_op jit(solution)/shard_map/ppermute | solution.py:20
  25.6 4.3 %scatter_custom_fusion.1 = s32[128]{0:T(128)S(1)} fusion(s32[1024]{0:T(1024)S(1)} %bitcast.84, s32[1024]{0:T(1024)S(1)} %ne.152, s32[]{:T(128)} %constant.136.clone.1), kind=kCustom, calls=%fused_computation.111 | custom fusion | bytes 516 | tf_op jit(solution)/shard_map/scatter | solution.py:83
  29.9 4.3 %scatter_custom_fusion = s32[128]{0:T(128)S(1)} fusion(s32[1024]{0:T(1024)S(1)} %bitcast.85, s32[1024]{0:T(1024)S(1)} %iota.26, s32[]{:T(128)} %constant.136.clone.1), kind=kCustom, calls=%fused_computation.113 | custom fusion | bytes 516 | tf_op jit(solution)/shard_map/scatter | solution.py:81
  36.3 7.6 %all-to-all-start = ((bf16[32,1,16]{2,1,0:T(2,128)(2,1)}), bf16[32,1,16]{2,1,0:T(2,128)(2,1)S(1)}, u32[]{:S(2)}, u32[]{:S(2)}) async-start(bf16[32,1,16]{2,1,0:T(2,128)(2,1)} %copy.26), calls=%async_computation | async-start | bytes 32768 | tf_op jit(solution)/shard_map/all_to_all | solution.py:103
  43.9 32.4 %all_gather.3 = bf16[128,2048]{1,0:T(8,128)(2,1)S(1)} all-gather(bf16[128,128]{1,0:T(8,128)(2,1)} %param.7), channel_id=1, replica_groups=mesh['dp'=32,'expert'=16] {'expert'}, dimensions={1}, use_global_device_ids=true | all-gather | bytes 557056 | tf_op jit(solution)/shard_map/all_gather | solution.py:62
  79.7 3.9 collective-permute-start.2
  83.7 3.1 collective-permute-start.5
  89.6 4.3 %collective-permute-start.7 = (bf16[128,128]{1,0:T(8,128)(2,1)S(1)}, bf16[128,128]{1,0:T(8,128)(2,1)S(1)}, u32[]{:S(2)}, u32[]{:S(2)}) collective-permute-start(bf16[128,128]{1,0:T(8,128)(2,1)S(1)} %collective-permute-done.5), channel_id=1, source_target_pairs={{0,15},{1,0},{2,1},{3,2},{4,3},{5,4},{6,5},{7,6},{8,7},{9,8},{10,9... | collective-permute-start | bytes 98312 | tf_op jit(solution)/shard_map/ppermute | solution.py:20
  96.0 5.1 %collective-permute-start.9 = (bf16[128,128]{1,0:T(8,128)(2,1)S(1)}, bf16[128,128]{1,0:T(8,128)(2,1)S(1)}, u32[]{:S(2)}, u32[]{:S(2)}) collective-permute-start(bf16[128,128]{1,0:T(8,128)(2,1)S(1)} %collective-permute-done.7), channel_id=1, source_target_pairs={{0,15},{1,0},{2,1},{3,2},{4,3},{5,4},{6,5},{7,6},{8,7},{9,8},{10,9... | collective-permute-start | bytes 98312 | tf_op jit(solution)/shard_map/ppermute | solution.py:20
  103.1 5.1 %collective-permute-start.11 = (bf16[128,128]{1,0:T(8,128)(2,1)S(1)}, bf16[128,128]{1,0:T(8,128)(2,1)S(1)}, u32[]{:S(2)}, u32[]{:S(2)}) collective-permute-start(bf16[128,128]{1,0:T(8,128)(2,1)S(1)} %collective-permute-done.9), channel_id=1, source_target_pairs={{0,15},{1,0},{2,1},{3,2},{4,3},{5,4},{6,5},{7,6},{8,7},{9,8},{10,9... | collective-permute-start | bytes 98312 | tf_op jit(solution)/shard_map/ppermute | solution.py:20
  110.2 5.1 %collective-permute-start.13 = (bf16[128,128]{1,0:T(8,128)(2,1)S(1)}, bf16[128,128]{1,0:T(8,128)(2,1)S(1)}, u32[]{:S(2)}, u32[]{:S(2)}) collective-permute-start(bf16[128,128]{1,0:T(8,128)(2,1)S(1)} %collective-permute-done.11), channel_id=1, source_target_pairs={{0,15},{1,0},{2,1},{3,2},{4,3},{5,4},{6,5},{7,6},{8,7},{9,8},{10,9... | collective-permute-start | bytes 98312 | tf_op jit(solution)/shard_map/ppermute | solution.py:20
  117.4 5.0 %collective-permute-done.12 = bf16[128,128]{1,0:T(8,128)(2,1)S(1)} collective-permute-done((bf16[128,128]{1,0:T(8,128)(2,1)S(1)}, bf16[128,128]{1,0:T(8,128)(2,1)S(1)}, u32[]{:S(2)}, u32[]{:S(2)}) %collective-permute-start.12) | collective-permute-done | bytes 32800 | tf_op jit(solution)/shard_map/ppermute | solution.py:17
  124.4 5.0 %collective-permute-done.14 = bf16[128,128]{1,0:T(8,128)(2,1)S(1)} collective-permute-done((bf16[128,128]{1,0:T(8,128)(2,1)S(1)}, bf16[128,128]{1,0:T(8,128)(2,1)S(1)}, u32[]{:S(2)}, u32[]{:S(2)}) %collective-permute-start.14) | collective-permute-done | bytes 32800 | tf_op jit(solution)/shard_map/ppermute | solution.py:17
  130.8 32.6 %all_to_all.36 = bf16[32,16,2048]{2,1,0:T(8,128)(2,1)S(1)} all-to-all(bf16[32,16,2048]{2,1,0:T(8,128)(2,1)S(1)} %bitcast.76), channel_id=1, replica_groups=mesh['dp'=32,'expert'=16] {'dp'}, dimensions={0} | all-to-all | bytes 4194304 | tf_op jit(solution)/shard_map/all_to_all | solution.py:102
  164.9 7.0 %all-to-all-start.3 = ((bf16[32,16,2048]{2,1,0:T(8,128)(2,1)}), bf16[32,16,2048]{2,1,0:T(8,128)(2,1)}, u32[]{:S(2)}, u32[]{:S(2)}) async-start(bf16[32,16,2048]{2,1,0:T(8,128)(2,1)} %bitcast.75), calls=%async_computation.4 | async-start | bytes 4194304 | tf_op jit(solution)/shard_map/all_to_all | solution.py:131
  176.5 21.4 %all-to-all-done.3 = bf16[32,16,2048]{2,1,0:T(8,128)(2,1)} async-done(((bf16[32,16,2048]{2,1,0:T(8,128)(2,1)}), bf16[32,16,2048]{2,1,0:T(8,128)(2,1)}, u32[]{:S(2)}, u32[]{:S(2)}) %all-to-all-start.3) | async-done | bytes 2097184 | tf_op jit(solution)/shard_map/all_to_all | solution.py:131
  203.4 7.7 %all-to-all-start.2 = ((bf16[32,16,2048]{2,1,0:T(8,128)(2,1)}), bf16[32,16,2048]{2,1,0:T(8,128)(2,1)}, u32[]{:S(2)}, u32[]{:S(2)}) async-start(bf16[32,16,2048]{2,1,0:T(8,128)(2,1)} %bitcast.79), calls=%async_computation.2 | async-start | bytes 4194304 | tf_op jit(solution)/shard_map/all_to_all | solution.py:112
  215.5 21.6 %all-to-all-done.2 = bf16[32,16,2048]{2,1,0:T(8,128)(2,1)} async-done(((bf16[32,16,2048]{2,1,0:T(8,128)(2,1)}), bf16[32,16,2048]{2,1,0:T(8,128)(2,1)}, u32[]{:S(2)}, u32[]{:S(2)}) %all-to-all-start.2) | async-done | bytes 2097184 | tf_op jit(solution)/shard_map/all_to_all | solution.py:112
  237.1 7.6 %all-to-all-start.4 = ((bf16[32,16,2048]{2,1,0:T(8,128)(2,1)}), bf16[32,16,2048]{2,1,0:T(8,128)(2,1)}, u32[]{:S(2)}, u32[]{:S(2)}) async-start(bf16[32,16,2048]{2,1,0:T(8,128)(2,1)} %bitcast.74), calls=%async_computation.5 | async-start | bytes 4194304 | tf_op jit(solution)/shard_map/all_to_all | solution.py:151
  247.9 22.8 %all-to-all-done.4 = bf16[32,16,2048]{2,1,0:T(8,128)(2,1)} async-done(((bf16[32,16,2048]{2,1,0:T(8,128)(2,1)}), bf16[32,16,2048]{2,1,0:T(8,128)(2,1)}, u32[]{:S(2)}, u32[]{:S(2)}) %all-to-all-start.4) | async-done | bytes 2097184 | tf_op jit(solution)/shard_map/all_to_all | solution.py:151
  276.5 6.8 %all-to-all-start.5 = ((bf16[32,1,16]{2,1,0:T(2,128)(2,1)}), bf16[32,1,16]{2,1,0:T(2,128)(2,1)S(1)}, u32[]{:S(2)}, u32[]{:S(2)}) async-start(bf16[32,1,16]{2,1,0:T(2,128)(2,1)} %convert_element_type.95), calls=%async_computation.7 | async-start | bytes 32768 | tf_op jit(solution)/shard_map/all_to_all | solution.py:158
  284.9 3.2 fusion.2
  292.2 52.7 %all-reduce = f32[128,8]{1,0:T(8,128)S(1)} all-reduce(f32[128,8]{1,0:T(8,128)S(1)} %bitcast.80), channel_id=4, replica_groups=mesh['dp'=32,'expert'=16] {'expert'}, use_global_device_ids=true, to_apply=%region_8.9.clone | all-reduce | flops 1024 | bytes 8192
  347.0 40.3 %reduce-scatter.5.cloned.1.call-done = f32[128,128]{1,0:T(8,128)} async-done(((f32[128,2048]{1,0:T(8,128)}), f32[128,128]{1,0:T(8,128)}) %reduce-scatter.5.cloned.1.call-update) | async-done | bytes 65552 | tf_op jit(solution)/shard_map/reduce_scatter | solution.py:174
  (122 shorter events, 59.3 us)
Async XLA Ops:
  7.2 190.7 %copy-start = (bf16[1,192,2048]{2,1,0:T(8,128)(2,1)S(1)}, bf16[1,192,2048]{2,1,0:T(8,128)(2,1)}, u32[]{:S(2)}) copy-start(bf16[1,192,2048]{2,1,0:T(8,128)(2,1)} %param.12) | copy-start | bytes 2359300
  7.2 69.2 %copy-start.3 = (bf16[128,128]{1,0:T(8,128)(2,1)S(1)}, bf16[128,128]{1,0:T(8,128)(2,1)}, u32[]{:S(2)}) copy-start(bf16[128,128]{1,0:T(8,128)(2,1)} %param.13) | copy-start | bytes 98308
  7.2 70.6 %collective-permute-start.1 = (bf16[128,128]{1,0:T(8,128)(2,1)}, bf16[128,128]{1,0:T(8,128)(2,1)S(1)}, u32[]{:S(2)}, u32[]{:S(2)}) collective-permute-start(bf16[128,128]{1,0:T(8,128)(2,1)} %param.13), channel_id=1, source_target_pairs={{0,15},{1,0},{2,1},{3,2},{4,3},{5,4},{6,5},{7,6},{8,7},{9,8},{10,9... | collective-permute-start | bytes 98312 | tf_op jit(solution)/shard_map/ppermute | solution.py:20
  18.7 61.0 %collective-permute-start = (bf16[128,128]{1,0:T(8,128)(2,1)}, bf16[128,128]{1,0:T(8,128)(2,1)S(1)}, u32[]{:S(2)}, u32[]{:S(2)}) collective-permute-start(bf16[128,128]{1,0:T(8,128)(2,1)} %param.13), channel_id=1, source_target_pairs={{0,1},{1,2},{2,3},{3,4},{4,5},{5,6},{6,7},{7,8},{8,9},{9,10},{10,1... | collective-permute-start | bytes 98312 | tf_op jit(solution)/shard_map/ppermute | solution.py:17
  36.3 94.2 %all-to-all-start = ((bf16[32,1,16]{2,1,0:T(2,128)(2,1)}), bf16[32,1,16]{2,1,0:T(2,128)(2,1)S(1)}, u32[]{:S(2)}, u32[]{:S(2)}) async-start(bf16[32,1,16]{2,1,0:T(2,128)(2,1)} %copy.26), calls=%async_computation | async-start | bytes 32768 | tf_op jit(solution)/shard_map/all_to_all | solution.py:103
  77.8 5.9 %collective-permute-start.3 = (bf16[128,128]{1,0:T(8,128)(2,1)S(1)}, bf16[128,128]{1,0:T(8,128)(2,1)S(1)}, u32[]{:S(2)}, u32[]{:S(2)}) collective-permute-start(bf16[128,128]{1,0:T(8,128)(2,1)S(1)} %collective-permute-done.1), channel_id=1, source_target_pairs={{0,15},{1,0},{2,1},{3,2},{4,3},{5,4},{6,5},{7,6},{8,7},{9,8},{10,9... | collective-permute-start | bytes 98312 | tf_op jit(solution)/shard_map/ppermute | solution.py:20
  79.7 7.1 %collective-permute-start.2 = (bf16[128,128]{1,0:T(8,128)(2,1)S(1)}, bf16[128,128]{1,0:T(8,128)(2,1)S(1)}, u32[]{:S(2)}, u32[]{:S(2)}) collective-permute-start(bf16[128,128]{1,0:T(8,128)(2,1)S(1)} %collective-permute-done), channel_id=1, source_target_pairs={{0,1},{1,2},{2,3},{3,4},{4,5},{5,6},{6,7},{7,8},{8,9},{9,10},{10,1... | collective-permute-start | bytes 98312 | tf_op jit(solution)/shard_map/ppermute | solution.py:17
  83.7 5.9 %collective-permute-start.5 = (bf16[128,128]{1,0:T(8,128)(2,1)S(1)}, bf16[128,128]{1,0:T(8,128)(2,1)S(1)}, u32[]{:S(2)}, u32[]{:S(2)}) collective-permute-start(bf16[128,128]{1,0:T(8,128)(2,1)S(1)} %collective-permute-done.3), channel_id=1, source_target_pairs={{0,15},{1,0},{2,1},{3,2},{4,3},{5,4},{6,5},{7,6},{8,7},{9,8},{10,9... | collective-permute-start | bytes 98312 | tf_op jit(solution)/shard_map/ppermute | solution.py:20
  86.8 7.1 %collective-permute-start.4 = (bf16[128,128]{1,0:T(8,128)(2,1)S(1)}, bf16[128,128]{1,0:T(8,128)(2,1)S(1)}, u32[]{:S(2)}, u32[]{:S(2)}) collective-permute-start(bf16[128,128]{1,0:T(8,128)(2,1)S(1)} %collective-permute-done.2), channel_id=1, source_target_pairs={{0,1},{1,2},{2,3},{3,4},{4,5},{5,6},{6,7},{7,8},{8,9},{9,10},{10,1... | collective-permute-start | bytes 98312 | tf_op jit(solution)/shard_map/ppermute | solution.py:17
  89.6 6.3 %collective-permute-start.7 = (bf16[128,128]{1,0:T(8,128)(2,1)S(1)}, bf16[128,128]{1,0:T(8,128)(2,1)S(1)}, u32[]{:S(2)}, u32[]{:S(2)}) collective-permute-start(bf16[128,128]{1,0:T(8,128)(2,1)S(1)} %collective-permute-done.5), channel_id=1, source_target_pairs={{0,15},{1,0},{2,1},{3,2},{4,3},{5,4},{6,5},{7,6},{8,7},{9,8},{10,9... | collective-permute-start | bytes 98312 | tf_op jit(solution)/shard_map/ppermute | solution.py:20
  94.0 7.1 %collective-permute-start.6 = (bf16[128,128]{1,0:T(8,128)(2,1)S(1)}, bf16[128,128]{1,0:T(8,128)(2,1)S(1)}, u32[]{:S(2)}, u32[]{:S(2)}) collective-permute-start(bf16[128,128]{1,0:T(8,128)(2,1)S(1)} %collective-permute-done.4), channel_id=1, source_target_pairs={{0,1},{1,2},{2,3},{3,4},{4,5},{5,6},{6,7},{7,8},{8,9},{9,10},{10,1... | collective-permute-start | bytes 98312 | tf_op jit(solution)/shard_map/ppermute | solution.py:17
  96.0 7.1 %collective-permute-start.9 = (bf16[128,128]{1,0:T(8,128)(2,1)S(1)}, bf16[128,128]{1,0:T(8,128)(2,1)S(1)}, u32[]{:S(2)}, u32[]{:S(2)}) collective-permute-start(bf16[128,128]{1,0:T(8,128)(2,1)S(1)} %collective-permute-done.7), channel_id=1, source_target_pairs={{0,15},{1,0},{2,1},{3,2},{4,3},{5,4},{6,5},{7,6},{8,7},{9,8},{10,9... | collective-permute-start | bytes 98312 | tf_op jit(solution)/shard_map/ppermute | solution.py:20
  101.1 7.1 %collective-permute-start.8 = (bf16[128,128]{1,0:T(8,128)(2,1)S(1)}, bf16[128,128]{1,0:T(8,128)(2,1)S(1)}, u32[]{:S(2)}, u32[]{:S(2)}) collective-permute-start(bf16[128,128]{1,0:T(8,128)(2,1)S(1)} %collective-permute-done.6), channel_id=1, source_target_pairs={{0,1},{1,2},{2,3},{3,4},{4,5},{5,6},{6,7},{7,8},{8,9},{9,10},{10,1... | collective-permute-start | bytes 98312 | tf_op jit(solution)/shard_map/ppermute | solution.py:17
  103.1 7.1 %collective-permute-start.11 = (bf16[128,128]{1,0:T(8,128)(2,1)S(1)}, bf16[128,128]{1,0:T(8,128)(2,1)S(1)}, u32[]{:S(2)}, u32[]{:S(2)}) collective-permute-start(bf16[128,128]{1,0:T(8,128)(2,1)S(1)} %collective-permute-done.9), channel_id=1, source_target_pairs={{0,15},{1,0},{2,1},{3,2},{4,3},{5,4},{6,5},{7,6},{8,7},{9,8},{10,9... | collective-permute-start | bytes 98312 | tf_op jit(solution)/shard_map/ppermute | solution.py:20
  108.3 7.1 %collective-permute-start.10 = (bf16[128,128]{1,0:T(8,128)(2,1)S(1)}, bf16[128,128]{1,0:T(8,128)(2,1)S(1)}, u32[]{:S(2)}, u32[]{:S(2)}) collective-permute-start(bf16[128,128]{1,0:T(8,128)(2,1)S(1)} %collective-permute-done.8), channel_id=1, source_target_pairs={{0,1},{1,2},{2,3},{3,4},{4,5},{5,6},{6,7},{7,8},{8,9},{9,10},{10,1... | collective-permute-start | bytes 98312 | tf_op jit(solution)/shard_map/ppermute | solution.py:17
  110.2 14.1 %collective-permute-start.13 = (bf16[128,128]{1,0:T(8,128)(2,1)S(1)}, bf16[128,128]{1,0:T(8,128)(2,1)S(1)}, u32[]{:S(2)}, u32[]{:S(2)}) collective-permute-start(bf16[128,128]{1,0:T(8,128)(2,1)S(1)} %collective-permute-done.11), channel_id=1, source_target_pairs={{0,15},{1,0},{2,1},{3,2},{4,3},{5,4},{6,5},{7,6},{8,7},{9,8},{10,9... | collective-permute-start | bytes 98312 | tf_op jit(solution)/shard_map/ppermute | solution.py:20
  115.4 7.0 %collective-permute-start.12 = (bf16[128,128]{1,0:T(8,128)(2,1)S(1)}, bf16[128,128]{1,0:T(8,128)(2,1)S(1)}, u32[]{:S(2)}, u32[]{:S(2)}) collective-permute-start(bf16[128,128]{1,0:T(8,128)(2,1)S(1)} %collective-permute-done.10), channel_id=1, source_target_pairs={{0,1},{1,2},{2,3},{3,4},{4,5},{5,6},{6,7},{7,8},{8,9},{9,10},{10,1... | collective-permute-start | bytes 98312 | tf_op jit(solution)/shard_map/ppermute | solution.py:17
  122.4 7.0 %collective-permute-start.14 = (bf16[128,128]{1,0:T(8,128)(2,1)S(1)}, bf16[128,128]{1,0:T(8,128)(2,1)S(1)}, u32[]{:S(2)}, u32[]{:S(2)}) collective-permute-start(bf16[128,128]{1,0:T(8,128)(2,1)S(1)} %collective-permute-done.12), channel_id=1, source_target_pairs={{0,1},{1,2},{2,3},{3,4},{4,5},{5,6},{6,7},{7,8},{8,9},{9,10},{10,1... | collective-permute-start | bytes 98312 | tf_op jit(solution)/shard_map/ppermute | solution.py:17
  164.9 33.0 %all-to-all-start.3 = ((bf16[32,16,2048]{2,1,0:T(8,128)(2,1)}), bf16[32,16,2048]{2,1,0:T(8,128)(2,1)}, u32[]{:S(2)}, u32[]{:S(2)}) async-start(bf16[32,16,2048]{2,1,0:T(8,128)(2,1)} %bitcast.75), calls=%async_computation.4 | async-start | bytes 4194304 | tf_op jit(solution)/shard_map/all_to_all | solution.py:131
  203.4 33.7 %all-to-all-start.2 = ((bf16[32,16,2048]{2,1,0:T(8,128)(2,1)}), bf16[32,16,2048]{2,1,0:T(8,128)(2,1)}, u32[]{:S(2)}, u32[]{:S(2)}) async-start(bf16[32,16,2048]{2,1,0:T(8,128)(2,1)} %bitcast.79), calls=%async_computation.2 | async-start | bytes 4194304 | tf_op jit(solution)/shard_map/all_to_all | solution.py:112
  237.1 33.6 %all-to-all-start.4 = ((bf16[32,16,2048]{2,1,0:T(8,128)(2,1)}), bf16[32,16,2048]{2,1,0:T(8,128)(2,1)}, u32[]{:S(2)}, u32[]{:S(2)}) async-start(bf16[32,16,2048]{2,1,0:T(8,128)(2,1)} %bitcast.74), calls=%async_computation.5 | async-start | bytes 4194304 | tf_op jit(solution)/shard_map/all_to_all | solution.py:151
  244.7 100.8 %reduce-scatter.3.cloned.1.call-start = ((), (), s32[]{:S(2)}) async-start(), calls=%async_computation.8 | async-start | bytes 1114112 | tf_op jit(solution)/shard_map/reduce_scatter | solution.py:173
  247.9 139.4 %reduce-scatter.5.cloned.1.call-start = ((), (), s32[]{:S(2)}) async-start(), calls=%async_computation.9 | async-start | bytes 1114112 | tf_op jit(solution)/shard_map/reduce_scatter | solution.py:174
  276.5 13.0 %all-to-all-start.5 = ((bf16[32,1,16]{2,1,0:T(2,128)(2,1)}), bf16[32,1,16]{2,1,0:T(2,128)(2,1)S(1)}, u32[]{:S(2)}, u32[]{:S(2)}) async-start(bf16[32,1,16]{2,1,0:T(2,128)(2,1)} %convert_element_type.95), calls=%async_computation.7 | async-start | bytes 32768 | tf_op jit(solution)/shard_map/all_to_all | solution.py:158
  (4 other events, 6.9 us)
Sparse Core Ops, SparseCore 0:
  248.3 67.0 reduce-scatter.2
  318.2 69.0 reduce-scatter.4
